TPU v7x, 256 devices: a whole 4x4x8 slice. The times are simulated.
256 devices in a mesh: req: 32 (over y, z_lo, core), tp: 8 (over x, z_hi).
Axes of the slice: x: 4, y: 4, z: 8 (z_hi: 2, z_lo: 4; z = z_hi * 4 + z_lo), core: 2. Of those that a mesh axis runs over, the one named last changes fastest.
Arguments:
- hidden_in: bfloat16 [8192, 2048], P('req', 'tp'), may hold values from -6 to 6
- embeds: bfloat16 [8192, 2048], P('req', 'tp'), may hold values from -6 to 6
- seg_ids: int32 [8192], replicated, may hold values from 0 to 15, never falling along the last dimension, each value on 1 to 2048 neighbouring positions
- mamba_gain: float32 [2048], replicated, may hold values from 0.5 to 1.5
- w_z: bfloat16 [2048, 2048], P(None, 'tp'), may hold values from -0.125 to 0.125
- w_x: bfloat16 [2048, 2048], P(None, 'tp'), may hold values from -0.125 to 0.125
- w_bc: bfloat16 [2048, 256], P('tp'), may hold values from -0.125 to 0.125
- w_dt: bfloat16 [2048, 32], P(None, 'tp'), may hold values from -0.125 to 0.125
- dt_bias: float32 [32], P('tp'), may hold values from -2 to 0
- decay_rate: float32 [32], P('tp'), may hold values from 0.0009765625 to 0.048828125
- conv_x: float32 [4, 2048], P(None, 'tp'), may hold values from -3 to 3
- conv_bc: float32 [4, 256], replicated, may hold values from -3 to 3
- skip_gain: float32 [32], P('tp'), may hold values from 0.5 to 1.5
- gate_gain: float32 [2048], P('tp'), may hold values from 0.5 to 1.5
- w_out: bfloat16 [2048, 2048], P('tp'), may hold values from -0.125 to 0.125
- attn_gain: float32 [4096], replicated, may hold values from 0.5 to 1.5
- w_qkv: bfloat16 [4096, 3, 2048], P(None, None, 'tp'), may hold values from -0.375 to 0.375
- adapter_down: bfloat16 [4096, 384], P('tp'), may hold values from -0.09375 to 0.09375
- adapter_up: bfloat16 [3, 128, 2048], P(None, None, 'tp'), may hold values from -0.5 to 0.5
- w_o: bfloat16 [2048, 2048], P('tp'), may hold values from -0.125 to 0.125
Outputs:
- hidden_out: bfloat16 [8192, 2048], P('req', 'tp')
- ssm_states: float32 [32, 32, 64, 128], P('req', 'tp')
- kv_cache: bfloat16 [8192, 2, 2048], P('req', None, 'tp')
Inputs may be any that keep to these rules, and one draw needn't show every extreme that they name: `seg_ids`: segment ids never fall; each of the 16 requests holds 1 to 2048 consecutive tokens and one holds exactly 2048.
All inputs are finite; a program needn't handle non-finite values.
Results may differ from a plain program's by a relative error of at most 0.013.
Values may be sent and summed in bfloat16 or wider, within the bound.
No kernel may reach another device: no remote copies, remote signals or barrier semaphores. Data moves between devices by JAX's collectives and lax.ppermute only.
A program may use at most 128 MiB of HBM per device.

v0:
```python
import math
import jax
import jax.numpy as jnp
from jax import lax
from jax.sharding import PartitionSpec as P

AHD = 128
highest = lax.Precision.HIGHEST
epsilon = 1e-05


def from_behind(block, axis, distance):
    devices = range(lax.axis_size(axis))
    route = [(i - distance, i) for i in devices if i - distance in devices]
    return lax.ppermute(block, axis, route)


def carried_in_2(value, axis, join, neutral):
    count, mine = (lax.axis_size(axis), lax.axis_index(axis))
    pieces = jax.tree.map(lambda part: lax.all_gather(part, axis), value)
    so_far = jax.tree.map(
        lambda part, zero: jnp.full_like(part, 0) + jnp.asarray(zero, part.dtype), value, neutral
    )

    def lap(position, so_far):
        longer = join(so_far, jax.tree.map(lambda part: part[position], pieces))
        return jax.tree.map(lambda new, old: jnp.where(position < mine, new, old), longer, so_far)

    return lax.fori_loop(0, count - 1, lap, so_far)


def rms_rows(values, gain):
    values = values.astype(jnp.float32)
    factor = lax.rsqrt(jnp.mean(values * values, axis=-1, keepdims=True) + epsilon)
    return values * factor * gain


def positions_of(seg_all):
    total_rows = seg_all.shape[0]
    indices = jnp.arange(total_rows, dtype=jnp.int32)
    begins = jnp.concatenate([jnp.ones((1,), dtype=bool), seg_all[1:] != seg_all[:-1]])
    first_index = lax.cummax(jnp.where(begins, indices, jnp.zeros_like(indices)), axis=0)
    return indices - first_index


def rotate(values, places):
    half_dim = values.shape[-1] // 2
    freqs = jnp.exp(-jnp.log(10000.0) * jnp.arange(half_dim, dtype=jnp.float32) / half_dim)
    angles = places.astype(jnp.float32)[:, None] * freqs[None, :]
    cosine = jnp.cos(angles)[:, None, :]
    sine = jnp.sin(angles)[:, None, :]
    first_half = values[..., :half_dim]
    second_half = values[..., half_dim:]
    return jnp.concatenate(
        [first_half * cosine - second_half * sine, second_half * cosine + first_half * sine],
        axis=-1,
    )


def conv_rows(extended, seg_extended, kernel, seg_now):
    kernel_len = kernel.shape[0]
    rows_out = seg_now.shape[0]
    result = jnp.zeros((rows_out, extended.shape[1]), jnp.float32)
    for offset in range(kernel_len):
        window_rows = extended[offset : offset + rows_out]
        matches = (seg_extended[offset : offset + rows_out] == seg_now)[:, None]
        result = result + jnp.where(matches, window_rows * kernel[offset][None, :], 0.0)
    return jax.nn.silu(result)


def ssd_block(
    inner, write_rows, read_rows, steps_dt, log_decay, seg_block, seg_before, state_prev, skip_gain
):
    length = inner.shape[0]
    cumul = jnp.cumsum(log_decay, axis=0)
    order = jnp.arange(length, dtype=jnp.int32)
    within = (seg_block[:, None] == seg_block[None, :]) & (order[:, None] >= order[None, :])
    spread = cumul.T[:, :, None] - cumul.T[:, None, :]
    decays = jnp.where(within[None], jnp.exp(jnp.minimum(spread, 0.0)), 0.0)
    intersection = jnp.dot(read_rows, write_rows.T, precision=highest)
    mixing = decays * intersection[None] * steps_dt.T[:, None, :]
    local_out = jnp.einsum("hts,shp->thp", mixing, inner, precision=highest)
    carried = jnp.where((seg_block == seg_before)[:, None], jnp.exp(cumul), 0.0)
    from_state = jnp.einsum("tn,hpn->thp", read_rows, state_prev, precision=highest)
    outputs = local_out + carried[:, :, None] * from_state + skip_gain[None, :, None] * inner
    tail_weight = (
        jnp.where((seg_block == seg_block[-1])[:, None], jnp.exp(cumul[-1][None, :] - cumul), 0.0)
        * steps_dt
    )
    keep_factor = jnp.where(seg_block[-1] == seg_before, jnp.exp(cumul[-1]), 0.0)
    state_next = keep_factor[:, None, None] * state_prev + jnp.einsum(
        "sh,shp,sn->hpn", tail_weight, inner, write_rows, precision=highest
    )
    return (outputs, state_next)


def accumulate_rows(left_rows, weight_rows):
    return jnp.dot(left_rows, weight_rows, preferred_element_type=jnp.float32)


def combine_states(earlier, later):
    return (earlier[0] * later[0], later[0][:, None, None] * earlier[1] + later[1])


def on_device(
    hidden_in,
    embeds,
    seg_ids,
    mamba_gain,
    w_z,
    w_x,
    w_bc,
    w_dt,
    dt_bias,
    decay_rate,
    conv_x,
    conv_bc,
    skip_gain,
    gate_gain,
    w_out,
    attn_gain,
    w_qkv,
    adapter_down,
    adapter_up,
    w_o,
):
    rows_here = hidden_in.shape[0]
    tensor_size = lax.axis_size("tp")
    req_rank = lax.axis_index("req")
    first_row = req_rank * rows_here
    full_hidden, full_embeds = (
        lax.all_gather(hidden_in, "tp", axis=1, tiled=True),
        lax.all_gather(embeds, "tp", axis=1, tiled=True),
    )
    normed = rms_rows(full_hidden, mamba_gain).astype(jnp.bfloat16)
    gate_z = jnp.dot(normed, w_z, preferred_element_type=jnp.float32)
    inner_x = jnp.dot(normed, w_x, preferred_element_type=jnp.float32)
    raw_dt = jnp.dot(normed, w_dt, preferred_element_type=jnp.float32)
    state_io = accumulate_rows(normed, lax.all_gather(w_bc, "tp", axis=0, tiled=True))
    mixed_in = jnp.concatenate([inner_x, state_io], axis=1)
    kernel_len = conv_x.shape[0]
    tail_rows = mixed_in[rows_here - (kernel_len - 1) :]
    prior_rows = from_behind(tail_rows, "req", 1)
    extended = jnp.concatenate([prior_rows, mixed_in], axis=0)
    seg_padded = jnp.concatenate(
        [jnp.full((kernel_len - 1,), -1, dtype=jnp.int32), seg_ids], axis=0
    )
    seg_extended = lax.dynamic_slice_in_dim(seg_padded, first_row, rows_here + kernel_len - 1, 0)
    seg_now = lax.dynamic_slice_in_dim(seg_ids, first_row, rows_here, 0)
    kernel = jnp.concatenate([conv_x, conv_bc], axis=1)
    conv_out = conv_rows(extended, seg_extended, kernel, seg_now)
    inner_here = w_z.shape[1]
    heads_here = w_dt.shape[1]
    head_dim = inner_here // heads_here
    state_dim = state_io.shape[1] // 2
    inner_c = conv_out[:, :inner_here].reshape(rows_here, heads_here, head_dim)
    write_rows = conv_out[:, inner_here : inner_here + state_dim]
    read_rows = conv_out[:, inner_here + state_dim :]
    steps_dt = jax.nn.softplus(raw_dt + dt_bias)
    log_decay = -steps_dt * decay_rate
    seg_before = jnp.where(req_rank > 0, seg_ids[jnp.maximum(first_row - 1, 0)], -1)
    seg_prior = jnp.concatenate([seg_before[None], seg_now[:-1]], axis=0)
    block_rows = math.gcd(rows_here, 256)
    count_blocks = rows_here // block_rows
    block_before = seg_prior.reshape(count_blocks, block_rows)[:, 0]

    def ssd_step(state_prev, pieces):
        blk_inner, blk_write, blk_read, blk_dt, blk_decay, blk_seg, blk_before = pieces
        outputs, state_next = ssd_block(
            blk_inner,
            blk_write,
            blk_read,
            blk_dt,
            blk_decay,
            blk_seg,
            blk_before,
            state_prev,
            skip_gain,
        )
        return (state_next, outputs)

    zero_state = jnp.zeros((heads_here, head_dim, state_dim), jnp.float32)
    local_state, local_out = lax.scan(
        ssd_step,
        zero_state,
        (
            inner_c.reshape(count_blocks, block_rows, heads_here, head_dim),
            write_rows.reshape(count_blocks, block_rows, state_dim),
            read_rows.reshape(count_blocks, block_rows, state_dim),
            steps_dt.reshape(count_blocks, block_rows, heads_here),
            log_decay.reshape(count_blocks, block_rows, heads_here),
            seg_now.reshape(count_blocks, block_rows),
            block_before,
        ),
    )
    local_out = local_out.reshape(rows_here, heads_here, head_dim)
    cumul_all = jnp.cumsum(log_decay, axis=0)
    through = jnp.where(seg_now[-1] == seg_before, jnp.exp(cumul_all[-1]), 0.0)
    incoming = carried_in_2(
        (through, local_state),
        "req",
        combine_states,
        (jnp.ones_like(through), jnp.zeros_like(local_state)),
    )
    carried_in = incoming[1]
    carried = jnp.where((seg_now == seg_before)[:, None], jnp.exp(cumul_all), 0.0)
    from_state = jnp.einsum("tn,hpn->thp", read_rows, carried_in, precision=highest)
    ssm_y = local_out + carried[:, :, None] * from_state
    final_state = local_state + through[:, None, None] * carried_in
    gated_rows = ssm_y.reshape(rows_here, inner_here) * jax.nn.silu(gate_z)
    square_sum = lax.psum(jnp.sum(gated_rows * gated_rows, axis=1), "tp")
    factor = lax.rsqrt(square_sum / (inner_here * tensor_size) + epsilon)
    gated_norm = (gated_rows * factor[:, None] * gate_gain).astype(jnp.bfloat16)
    mix_terms = jnp.dot(gated_norm, w_out, preferred_element_type=jnp.float32)
    mix_share = lax.psum_scatter(mix_terms, "tp", scatter_dimension=1, tiled=True)
    mid_here = (hidden_in.astype(jnp.float32) + mix_share).astype(jnp.bfloat16)
    mid_full = lax.all_gather(mid_here, "tp", axis=1, tiled=True)
    joined = jnp.concatenate([mid_full, full_embeds], axis=1)
    attn_in = rms_rows(joined, attn_gain).astype(jnp.bfloat16)
    low_sum = accumulate_rows(attn_in, lax.all_gather(adapter_down, "tp", axis=0, tiled=True))
    low_rank = low_sum.astype(jnp.bfloat16)
    rank_cols = adapter_up.shape[1]
    cols_here = w_qkv.shape[2]
    heads_attn = cols_here // AHD
    projected = jnp.dot(
        attn_in, w_qkv.reshape(w_qkv.shape[0], 3 * cols_here), preferred_element_type=jnp.float32
    ).reshape(rows_here, 3, cols_here)
    projected = projected + jnp.einsum(
        "tjr,jrc->tjc",
        low_rank.reshape(rows_here, 3, rank_cols),
        adapter_up,
        preferred_element_type=jnp.float32,
    )
    places = lax.dynamic_slice_in_dim(positions_of(seg_ids), first_row, rows_here, 0)
    queries = rotate(projected[:, 0].reshape(rows_here, heads_attn, AHD), places).astype(
        jnp.bfloat16
    )
    key_rows = rotate(projected[:, 1].reshape(rows_here, heads_attn, AHD), places).astype(
        jnp.bfloat16
    )
    value_rows = projected[:, 2].astype(jnp.bfloat16)
    kv_pair = jnp.stack([key_rows.reshape(rows_here, cols_here), value_rows], axis=1)
    query_index = first_row + jnp.arange(rows_here, dtype=jnp.int32)
    inv_root = 1.0 / math.sqrt(AHD)

    def absorb(running, block_kv, first_key):
        row_top, denom_sum, weighted = running
        key_count = block_kv.shape[0]
        key_index = first_key + jnp.arange(key_count, dtype=jnp.int32)
        key_seg = lax.dynamic_slice_in_dim(seg_ids, jnp.maximum(first_key, 0), key_count, 0)
        allowed = (
            (key_seg[None, :] == seg_now[:, None])
            & (key_index[None, :] <= query_index[:, None])
            & (key_index[None, :] >= 0)
        )
        block_keys = block_kv[:, 0].reshape(key_count, heads_attn, AHD)
        block_vals = block_kv[:, 1].reshape(key_count, heads_attn, AHD)
        scores = (
            jnp.einsum("qhe,khe->hqk", queries, block_keys, preferred_element_type=jnp.float32)
            * inv_root
        )
        masked = jnp.where(allowed[None], scores, -1e30)
        new_top = jnp.maximum(row_top, jnp.max(masked, axis=-1))
        weights = jnp.where(allowed[None], jnp.exp(scores - new_top[:, :, None]), 0.0)
        shrink = jnp.exp(row_top - new_top)
        denom_sum = denom_sum * shrink + jnp.sum(weights, axis=-1)
        weighted = weighted * shrink[:, :, None] + jnp.einsum(
            "hqk,khe->hqe",
            weights.astype(jnp.bfloat16),
            block_vals,
            preferred_element_type=jnp.float32,
        )
        return (new_top, denom_sum, weighted)

    start_state = (
        jnp.full((heads_attn, rows_here), -1e30, jnp.float32),
        jnp.zeros((heads_attn, rows_here), jnp.float32),
        jnp.zeros((heads_attn, rows_here, AHD), jnp.float32),
    )
    reach_hops = lax.axis_size("req") // 4
    running = absorb(start_state, kv_pair, first_row)
    moving = kv_pair
    for hop_count in range(1, reach_hops + 1):
        moving = from_behind(moving, "req", 1)
        running = absorb(running, moving, first_row - hop_count * rows_here)
    row_top, denom_sum, weighted = running
    attended = (weighted / denom_sum[:, :, None]).astype(jnp.bfloat16)
    attended = attended.transpose(1, 0, 2).reshape(rows_here, cols_here)
    attn_terms = jnp.dot(attended, w_o, preferred_element_type=jnp.float32)
    attn_share = lax.psum_scatter(
        attn_terms.astype(jnp.bfloat16), "tp", scatter_dimension=1, tiled=True
    ).astype(jnp.float32)
    hidden_out = (mid_here.astype(jnp.float32) + attn_share).astype(jnp.bfloat16)
    return (hidden_out, final_state[None], kv_pair)


def solution(mesh):
    in_specs = (
        P("req", "tp"),
        P("req", "tp"),
        P(),
        P(),
        P(None, "tp"),
        P(None, "tp"),
        P("tp", None),
        P(None, "tp"),
        P("tp"),
        P("tp"),
        P(None, "tp"),
        P(),
        P("tp"),
        P("tp"),
        P("tp", None),
        P(),
        P(None, None, "tp"),
        P("tp", None),
        P(None, None, "tp"),
        P("tp", None),
    )
    out_specs = (P("req", "tp"), P("req", "tp", None, None), P("req", None, "tp"))
    return jax.shard_map(
        on_device, mesh=mesh, in_specs=in_specs, out_specs=out_specs, check_vma=False
    )
```

profile of v0, /device:TPU:8, one launch (start us, length us, event | category | flops | bytes accessed | tf_op | source)
XLA Modules:
  0.0 785.6 jit_solution(5551168740319205681)
XLA Ops:
  8.7 1.3 dynamic_slice.74
  16.7 1.4 broadcast_compare_fusion.9
  18.1 56.8 %all-gather.9.cloned.1.call-done = bf16[256,2048]{1,0:T(8,128)(2,1)} async-done(((bf16[256,256]{1,0:T(8,128)(2,1)}), bf16[256,2048]{1,0:T(8,128)(2,1)}) %all-gather.9.cloned.1.call-update) | async-done | bytes 1048592 | tf_op jit(solution)/shard_map/all_gather | solution.py:132
  74.9 1.6 fusion.6
  76.5 58.3 %all-gather.11.cloned.1.call-done = bf16[2048,256]{1,0:T(8,128)(2,1)} async-done(((bf16[256,256]{1,0:T(8,128)(2,1)}), bf16[2048,256]{1,0:T(8,128)(2,1)}) %all-gather.11.cloned.1.call-update) | async-done | bytes 1048592 | tf_op jit(solution)/shard_map/all_gather | solution.py:139
  134.8 2.2 fusion.161
  137.1 1.9 fusion.163
  139.1 1.9 collective-permute-start
  141.1 1.1 negate_multiply_fusion
  142.2 1.2 reduce-window.19
  145.2 4.3 collective-permute-done
  150.5 1.0 convolution_add_fusion
  151.8 1.7 fusion.181
  153.5 1.9 and_and_fusion.6
  156.2 34.6 %all-gather.1 = f32[32,1,4]{2,1,0:T(1,128)} all-gather(f32[1,1,4]{2,1,0:T(1,128)} %bitcast.388), channel_id=1, replica_groups=mesh['req'=32,'tp'=8] {'req'}, dimensions={0}, use_global_device_ids=true | all-gather | bytes 528 | tf_op jit(solution)/shard_map/all_gather | solution.py:20
  191.2 2.2 convolution_bitcast_fusion.10
  193.4 1.0 fusion.31
  194.4 15.0 %all-gather.19.cloned.1.call-done = f32[128,64,128]{2,1,0:T(8,128)} async-done(((f32[4,64,128]{2,1,0:T(8,128)}), f32[128,64,128]{2,1,0:T(8,128)}) %all-gather.19.cloned.1.call-update) | async-done | bytes 4194320 | tf_op jit(solution)/shard_map/all_gather | solution.py:20
  209.4 52.5 %while.9 = (s32[]{:T(128)}, f32[4,64,128]{2,1,0:T(8,128)S(1)}, s32[]{:T(128)}, f32[32,4]{1,0:T(8,128)}, f32[32,4,64,128]{3,2,1,0:T(8,128)}, /*index=5*/s32[]{:T(128)}, s32[]{:T(128)}) while((s32[]{:T(128)}, f32[4,64,128]{2,1,0:T(8,128)S(1)}, s32[]{:T(128)}, f32[32,4]{1,0:T(8,128)}, f32[32,4,64,128]{3,2,1,0:T(8,128)}, ...), condition=%wide.region_4.5_spmd.clone, body=%wide.region_3.4_spmd.clone.sunk | while | flops 131076 | bytes 393369 | solution.py:29
  210.1 1.0 fusion.223
  211.8 1.0 fusion.223
  213.5 1.0 fusion.223
  215.2 1.0 fusion.223
  216.9 1.0 fusion.223
  218.5 1.0 fusion.223
  220.2 1.0 fusion.223
  221.9 1.0 fusion.223
  223.6 1.0 fusion.223
  225.3 1.0 fusion.223
  227.0 1.0 fusion.223
  228.7 1.0 fusion.223
  245.6 1.0 fusion.223
  259.2 1.0 fusion.223
  262.3 1.9 multiply_reduce_fusion
  264.2 29.9 %psum.7 = f32[256]{0:T(256)S(1)} all-reduce(f32[256]{0:T(256)S(1)} %get-tuple-element.279), channel_id=1, replica_groups=mesh['req'=32,'tp'=8] {'tp'}, use_global_device_ids=true, to_apply=%region_6.7 | all-reduce | flops 256 | bytes 2048 | tf_op jit(solution)/shard_map/psum | solution.py:211
  294.1 1.9 fusion.110
  296.7 89.3 %reduce-scatter.3.cloned.1.call-done = f32[256,256]{1,0:T(8,128)} async-done(((f32[256,2048]{1,0:T(8,128)}), f32[256,256]{1,0:T(8,128)}) %reduce-scatter.3.cloned.1.call-update) | async-done | bytes 262160 | tf_op jit(solution)/shard_map/reduce_scatter | solution.py:215
  386.0 1.6 add_convert_fusion.2
  388.6 8.8 %copy.99 = bf16[4096,3,256]{0,2,1:T(8,128)(2,1)} copy(bf16[4096,3,256]{2,0,1:T(8,128)(2,1)} %param.38) | data formatting | bytes 12582912 | tf_op args[16]
  399.5 46.1 %all-gather.15.cloned.1.call-done = bf16[256,2048]{1,0:T(8,128)(2,1)} async-done(((bf16[256,256]{1,0:T(8,128)(2,1)}), bf16[256,2048]{1,0:T(8,128)(2,1)}) %all-gather.15.cloned.1.call-update) | async-done | bytes 1048592 | tf_op jit(solution)/shard_map/all_gather | solution.py:133
  445.6 60.0 %all-gather.13.cloned.1.call-done = bf16[256,2048]{1,0:T(8,128)(2,1)} async-done(((bf16[256,256]{1,0:T(8,128)(2,1)}), bf16[256,2048]{1,0:T(8,128)(2,1)}) %all-gather.13.cloned.1.call-update) | async-done | bytes 1048592 | tf_op jit(solution)/shard_map/all_gather | solution.py:217
  505.6 2.0 fusion.3
  507.7 87.6 %all-gather.17.cloned.1.call-done = bf16[4096,384]{1,0:T(8,128)(2,1)} async-done(((bf16[512,384]{1,0:T(8,128)(2,1)}), bf16[4096,384]{1,0:T(8,128)(2,1)}) %all-gather.17.cloned.1.call-update) | async-done | bytes 3145744 | tf_op jit(solution)/shard_map/all_gather | solution.py:220
  595.3 3.5 convolution_convert_fusion.1
  599.0 5.1 fusion.1
  605.1 1.9 collective-permute-start.1
  607.8 7.8 collective-permute-done.1
  615.6 1.9 collective-permute-start.2
  618.8 7.4 collective-permute-done.2
  626.2 1.9 collective-permute-start.3
  628.4 8.1 %collective-permute-done.3 = bf16[256,2,256]{0,2,1:T(8,128)(2,1)S(1)} collective-permute-done((bf16[256,2,256]{0,2,1:T(8,128)(2,1)S(1)}, bf16[256,2,256]{0,2,1:T(8,128)(2,1)S(1)}, u32[]{:S(2)}, u32[]{:S(2)}) %collective-permute-start.3) | collective-permute-done | bytes 262176 | tf_op jit(solution)/shard_map/ppermute | solution.py:15
  636.6 1.9 collective-permute-start.4
  638.8 8.1 %collective-permute-done.4 = bf16[256,2,256]{0,2,1:T(8,128)(2,1)S(1)} collective-permute-done((bf16[256,2,256]{0,2,1:T(8,128)(2,1)S(1)}, bf16[256,2,256]{0,2,1:T(8,128)(2,1)S(1)}, u32[]{:S(2)}, u32[]{:S(2)}) %collective-permute-start.4) | collective-permute-done | bytes 262176 | tf_op jit(solution)/shard_map/ppermute | solution.py:15
  647.0 1.9 collective-permute-start.5
  649.2 8.1 %collective-permute-done.5 = bf16[256,2,256]{0,2,1:T(8,128)(2,1)S(1)} collective-permute-done((bf16[256,2,256]{0,2,1:T(8,128)(2,1)S(1)}, bf16[256,2,256]{0,2,1:T(8,128)(2,1)S(1)}, u32[]{:S(2)}, u32[]{:S(2)}) %collective-permute-start.5) | collective-permute-done | bytes 262176 | tf_op jit(solution)/shard_map/ppermute | solution.py:15
  657.3 1.9 collective-permute-start.6
  659.6 8.1 %collective-permute-done.6 = bf16[256,2,256]{0,2,1:T(8,128)(2,1)S(1)} collective-permute-done((bf16[256,2,256]{0,2,1:T(8,128)(2,1)S(1)}, bf16[256,2,256]{0,2,1:T(8,128)(2,1)S(1)}, u32[]{:S(2)}, u32[]{:S(2)}) %collective-permute-start.6) | collective-permute-done | bytes 262176 | tf_op jit(solution)/shard_map/ppermute | solution.py:15
  667.7 1.9 collective-permute-start.7
  670.0 8.1 %collective-permute-done.7 = bf16[256,2,256]{0,2,1:T(8,128)(2,1)S(1)} collective-permute-done((bf16[256,2,256]{0,2,1:T(8,128)(2,1)S(1)}, bf16[256,2,256]{0,2,1:T(8,128)(2,1)S(1)}, u32[]{:S(2)}, u32[]{:S(2)}) %collective-permute-start.7) | collective-permute-done | bytes 262176 | tf_op jit(solution)/shard_map/ppermute | solution.py:15
  678.1 1.9 collective-permute-start.8
  680.3 8.1 %collective-permute-done.8 = bf16[256,2,256]{0,2,1:T(8,128)(2,1)S(1)} collective-permute-done((bf16[256,2,256]{0,2,1:T(8,128)(2,1)S(1)}, bf16[256,2,256]{0,2,1:T(8,128)(2,1)S(1)}, u32[]{:S(2)}, u32[]{:S(2)}) %collective-permute-start.8) | collective-permute-done | bytes 262176 | tf_op jit(solution)/shard_map/ppermute | solution.py:15
  692.6 1.4 convolution_convert_fusion
  695.7 81.5 %reduce-scatter.5.cloned.1.call-done = bf16[256,256]{1,0:T(8,128)(2,1)} async-done(((bf16[256,2048]{1,0:T(8,128)(2,1)}), bf16[256,256]{1,0:T(8,128)(2,1)}) %reduce-scatter.5.cloned.1.call-update) | async-done | bytes 131088 | tf_op jit(solution)/shard_map/reduce_scatter | solution.py:290
  777.2 1.6 add_convert_fusion
  (221 shorter events, 62.5 us)
Async XLA Ops:
  7.2 287.0 %copy-start = (bf16[256,2048]{1,0:T(8,128)(2,1)S(1)}, bf16[256,2048]{1,0:T(8,128)(2,1)}, u32[]{:S(2)}) copy-start(bf16[256,2048]{1,0:T(8,128)(2,1)} %param.36) | copy-start | bytes 3145732
  7.2 67.7 %all-gather.9.cloned.1.call-start = ((), (), s32[]{:S(2)}) async-start(), calls=%async_computation.2 | async-start | bytes 1179648 | tf_op jit(solution)/shard_map/all_gather | solution.py:132
  7.9 129.1 %copy-start.20 = (f32[2048]{0:T(1024)S(1)}, f32[2048]{0:T(1024)}, u32[]{:S(2)}) copy-start(f32[2048]{0:T(1024)} %param.25) | copy-start | bytes 24580
  7.9 126.9 %all-gather.11.cloned.1.call-start = ((), (), s32[]{:S(2)}) async-start(), calls=%async_computation.3 | async-start | bytes 1179648 | tf_op jit(solution)/shard_map/all_gather | solution.py:139
  8.7 200.7 %all-gather.19.cloned.1.call-start = ((), (), s32[]{:S(2)}) async-start(), calls=%async_computation.9 | async-start | bytes 4325376 | tf_op jit(solution)/shard_map/all_gather | solution.py:20
  74.9 62.2 %copy-start.3 = (bf16[256,2048]{1,0:T(8,128)(2,1)S(1)}, bf16[256,2048]{1,0:T(8,128)(2,1)}, u32[]{:S(2)}) copy-start(bf16[256,2048]{1,0:T(8,128)(2,1)} %all-gather.9.cloned.1.call-done) | copy-start | bytes 3145732
  76.5 64.6 %copy-start.17 = (f32[256]{0:T(256)}, f32[256]{0:T(256)S(1)}, u32[]{:S(2)}) copy-start(f32[256]{0:T(256)S(1)} %add_rsqrt_fusion.2) | copy-start | bytes 3076
  137.1 4.0 copy-start.18
  137.1 4.0 copy-start.21
  137.1 4.0 copy-start.22
  139.1 10.4 %collective-permute-start = (f32[3,512]{0,1:T(8,128)S(1)}, f32[3,512]{0,1:T(8,128)S(1)}, u32[]{:S(2)}, u32[]{:S(2)}) collective-permute-start(f32[3,512]{0,1:T(8,128)S(1)} %fusion.80), channel_id=1, source_target_pairs={{0,8},{8,16},{16,24},{24,32},{32,40},{40,48},{48,56},{56,64},{64,7... | collective-permute-start | bytes 18440 | tf_op jit(solution)/shard_map/ppermute | solution.py:15
  143.8 0.7 copy-start.11
  151.5 234.4 %reduce-scatter.3.cloned.1.call-start = ((), (), s32[]{:S(2)}) async-start(), calls=%async_computation.4 | async-start | bytes 2359296 | tf_op jit(solution)/shard_map/reduce_scatter | solution.py:215
  262.3 31.9 %copy-start.16 = (f32[256]{0:T(256)S(1)}, f32[256]{0:T(256)}, u32[]{:S(2)}) copy-start(f32[256]{0:T(256)} %param.35) | copy-start | bytes 3076
  294.1 91.8 %copy-start.8 = (bf16[256,256]{1,0:T(8,128)(2,1)S(1)}, bf16[256,256]{1,0:T(8,128)(2,1)}, u32[]{:S(2)}) copy-start(bf16[256,256]{1,0:T(8,128)(2,1)} %param.22) | copy-start | bytes 393220
  296.1 149.5 %all-gather.15.cloned.1.call-start = ((), (), s32[]{:S(2)}) async-start(), calls=%async_computation.6 | async-start | bytes 1179648 | tf_op jit(solution)/shard_map/all_gather | solution.py:133
  296.6 209.0 %all-gather.13.cloned.1.call-start = ((), (), s32[]{:S(2)}) async-start(), calls=%async_computation.5 | async-start | bytes 1179648 | tf_op jit(solution)/shard_map/all_gather | solution.py:217
  387.6 207.7 %all-gather.17.cloned.1.call-start = ((), (), s32[]{:S(2)}) async-start(), calls=%async_computation.7 | async-start | bytes 3538944 | tf_op jit(solution)/shard_map/all_gather | solution.py:220
  388.4 9.1 %copy-start.9 = (s32[8192]{0:T(1024)S(1)}, s32[8192]{0:T(1024)}, u32[]{:S(2)}) copy-start(s32[8192]{0:T(1024)} %param.24) | copy-start | bytes 98308
  388.4 10.1 %copy-start.12 = (s32[256]{0:T(256)S(1)}, s32[256]{0:T(256)}, u32[]{:S(2)}) copy-start(s32[256]{0:T(256)} %get-tuple-element.235) | copy-start | bytes 3076
  388.4 10.1 %copy-start.13 = (s32[256]{0:T(256)S(1)}, s32[256]{0:T(256)}, u32[]{:S(2)}) copy-start(s32[256]{0:T(256)} %get-tuple-element.238) | copy-start | bytes 3076
  388.4 10.1 %copy-start.14 = (s32[256]{0:T(256)S(1)}, s32[256]{0:T(256)}, u32[]{:S(2)}) copy-start(s32[256]{0:T(256)} %get-tuple-element.239) | copy-start | bytes 3076
  388.4 388.8 %reduce-scatter.5.cloned.1.call-start = ((), (), s32[]{:S(2)}) async-start(), calls=%async_computation.8 | async-start | bytes 1179648 | tf_op jit(solution)/shard_map/reduce_scatter | solution.py:290
  397.4 197.9 %copy-start.19 = (f32[4096]{0:T(1024)S(1)}, f32[4096]{0:T(1024)}, u32[]{:S(2)}) copy-start(f32[4096]{0:T(1024)} %param.37) | copy-start | bytes 49156
  445.6 149.7 %copy-start.5 = (bf16[256,2048]{1,0:T(8,128)(2,1)S(1)}, bf16[256,2048]{1,0:T(8,128)(2,1)}, u32[]{:S(2)}) copy-start(bf16[256,2048]{1,0:T(8,128)(2,1)} %all-gather.15.cloned.1.call-done) | copy-start | bytes 3145732
  599.0 5.1 copy-start.10
  604.8 2.7 copy-start.7
  605.1 10.5 %collective-permute-start.1 = (bf16[256,2,256]{0,2,1:T(8,128)(2,1)S(1)}, bf16[256,2,256]{0,2,1:T(8,128)(2,1)}, u32[]{:S(2)}, u32[]{:S(2)}) collective-permute-start(bf16[256,2,256]{0,2,1:T(8,128)(2,1)S(1)} %pad_maximum_fusion.2), channel_id=1, source_target_pairs={{0,8},{8,16},{16,24},{24,32},{32,40},{40,48},{48,56},{56,64},{64,7... | collective-permute-start | bytes 786440 | tf_op jit(solution)/shard_map/ppermute | solution.py:15
  607.3 20.8 %copy-start.6 = (pred[256,256]{0,1:T(8,128)(4,1)S(1)}, pred[256,256]{0,1:T(8,128)(4,1)}, u32[]{:S(2)}) copy-start(pred[256,256]{0,1:T(8,128)(4,1)} %get-tuple-element.258) | copy-start | bytes 196612
  615.6 10.6 %collective-permute-start.2 = (bf16[256,2,256]{0,2,1:T(8,128)(2,1)}, bf16[256,2,256]{0,2,1:T(8,128)(2,1)S(1)}, u32[]{:S(2)}, u32[]{:S(2)}) collective-permute-start(bf16[256,2,256]{0,2,1:T(8,128)(2,1)} %collective-permute-done.1), channel_id=1, source_target_pairs={{0,8},{8,16},{16,24},{24,32},{32,40},{40,48},{48,56},{56,64},{64,7... | collective-permute-start | bytes 786440 | tf_op jit(solution)/shard_map/ppermute | solution.py:15
  626.2 10.4 %collective-permute-start.3 = (bf16[256,2,256]{0,2,1:T(8,128)(2,1)S(1)}, bf16[256,2,256]{0,2,1:T(8,128)(2,1)S(1)}, u32[]{:S(2)}, u32[]{:S(2)}) collective-permute-start(bf16[256,2,256]{0,2,1:T(8,128)(2,1)S(1)} %collective-permute-done.2), channel_id=1, source_target_pairs={{0,8},{8,16},{16,24},{24,32},{32,40},{40,48},{48,56},{56,64},{64,7... | collective-permute-start | bytes 786440 | tf_op jit(solution)/shard_map/ppermute | solution.py:15
  636.6 10.4 %collective-permute-start.4 = (bf16[256,2,256]{0,2,1:T(8,128)(2,1)S(1)}, bf16[256,2,256]{0,2,1:T(8,128)(2,1)S(1)}, u32[]{:S(2)}, u32[]{:S(2)}) collective-permute-start(bf16[256,2,256]{0,2,1:T(8,128)(2,1)S(1)} %collective-permute-done.3), channel_id=1, source_target_pairs={{0,8},{8,16},{16,24},{24,32},{32,40},{40,48},{48,56},{56,64},{64,7... | collective-permute-start | bytes 786440 | tf_op jit(solution)/shard_map/ppermute | solution.py:15
  647.0 10.4 %collective-permute-start.5 = (bf16[256,2,256]{0,2,1:T(8,128)(2,1)S(1)}, bf16[256,2,256]{0,2,1:T(8,128)(2,1)S(1)}, u32[]{:S(2)}, u32[]{:S(2)}) collective-permute-start(bf16[256,2,256]{0,2,1:T(8,128)(2,1)S(1)} %collective-permute-done.4), channel_id=1, source_target_pairs={{0,8},{8,16},{16,24},{24,32},{32,40},{40,48},{48,56},{56,64},{64,7... | collective-permute-start | bytes 786440 | tf_op jit(solution)/shard_map/ppermute | solution.py:15
  657.3 10.4 %collective-permute-start.6 = (bf16[256,2,256]{0,2,1:T(8,128)(2,1)S(1)}, bf16[256,2,256]{0,2,1:T(8,128)(2,1)S(1)}, u32[]{:S(2)}, u32[]{:S(2)}) collective-permute-start(bf16[256,2,256]{0,2,1:T(8,128)(2,1)S(1)} %collective-permute-done.5), channel_id=1, source_target_pairs={{0,8},{8,16},{16,24},{24,32},{32,40},{40,48},{48,56},{56,64},{64,7... | collective-permute-start | bytes 786440 | tf_op jit(solution)/shard_map/ppermute | solution.py:15
  667.7 10.4 %collective-permute-start.7 = (bf16[256,2,256]{0,2,1:T(8,128)(2,1)S(1)}, bf16[256,2,256]{0,2,1:T(8,128)(2,1)S(1)}, u32[]{:S(2)}, u32[]{:S(2)}) collective-permute-start(bf16[256,2,256]{0,2,1:T(8,128)(2,1)S(1)} %collective-permute-done.6), channel_id=1, source_target_pairs={{0,8},{8,16},{16,24},{24,32},{32,40},{40,48},{48,56},{56,64},{64,7... | collective-permute-start | bytes 786440 | tf_op jit(solution)/shard_map/ppermute | solution.py:15
  678.1 10.4 %collective-permute-start.8 = (bf16[256,2,256]{0,2,1:T(8,128)(2,1)S(1)}, bf16[256,2,256]{0,2,1:T(8,128)(2,1)S(1)}, u32[]{:S(2)}, u32[]{:S(2)}) collective-permute-start(bf16[256,2,256]{0,2,1:T(8,128)(2,1)S(1)} %collective-permute-done.7), channel_id=1, source_target_pairs={{0,8},{8,16},{16,24},{24,32},{32,40},{40,48},{48,56},{56,64},{64,7... | collective-permute-start | bytes 786440 | tf_op jit(solution)/shard_map/ppermute | solution.py:15
  691.4 1.2 copy-start.4
  691.9 2.2 copy-start.1
  691.9 2.2 copy-start.15
  692.6 84.5 %copy-start.2 = (bf16[256,256]{1,0:T(8,128)(2,1)S(1)}, bf16[256,256]{1,0:T(8,128)(2,1)}, u32[]{:S(2)}) copy-start(bf16[256,256]{1,0:T(8,128)(2,1)} %add_convert_fusion.2) | copy-start | bytes 393220
Sparse Core Ops, SparseCore 0:
  10.5 64.3 all-gather.8
  77.5 57.2 all-gather.10
  151.6 57.7 all-gather.18
  296.2 89.7 reduce-scatter.2
  388.3 57.2 all-gather.14
  448.5 57.0 all-gather.12
  508.2 87.0 all-gather.16
  694.2 82.9 reduce-scatter.4
where the time goes:
time: 788 us; the launch traced here: 786 us
  waiting for transfers between devices  566 us (72%)
  blocking collectives  64.5 us (8%)
  other arithmetic  49.5 us (6%)
  local copies, waits for them, and re-layouts  41 us (5%)
  matrix products  29.1 us (4%)
  starting transfers between devices  17.7 us (2%)
  between operations  17.7 us (2%)
    reduce_scatter x1, waiting for transfers between devices, on_device(): lax.psum_scatter(mix_terms, 'tp', scatter_dimension=1, tiled=True)  89.3 us
    all_gather x1, waiting for transfers between devices, on_device(): lax.all_gather(adapter_down, 'tp', axis=0, tiled=True)  87.6 us
    reduce_scatter x1, waiting for transfers between devices, on_device(): lax.psum_scatter(attn_terms.astype(jnp.bfloat16), 'tp', scatter_dimension...  81.5 us
    ppermute x9, waiting for transfers between devices, from_behind(): return lax.ppermute(block, axis, route)  68.4 us
    all_gather x1, waiting for transfers between devices, on_device(): mid_full = lax.all_gather(mid_here, 'tp', axis=1, tiled=True)  60 us
    all_gather x1, waiting for transfers between devices, on_device(): lax.all_gather(w_bc, 'tp', axis=0, tiled=True)  58.3 us
    all_gather x1, waiting for transfers between devices, on_device(): lax.all_gather(hidden_in, 'tp', axis=1, tiled=True)  56.8 us
    all_gather x1, waiting for transfers between devices, on_device(): lax.all_gather(embeds, 'tp', axis=1, tiled=True)  46.1 us
  transfers between devices with their start and end apart: 17, of which 17 were waited for; matrix products, arithmetic and copies ran while one was open for 5% of the time, Pallas kernels for 0%

commit v1 on v0

--- a/solution.py
+++ b/solution.py
@@ -214,7 +214,10 @@
     mix_terms = jnp.dot(gated_norm, w_out, preferred_element_type=jnp.float32)
     mix_share = lax.psum_scatter(mix_terms, "tp", scatter_dimension=1, tiled=True)
     mid_here = (hidden_in.astype(jnp.float32) + mix_share).astype(jnp.bfloat16)
-    mid_full = lax.all_gather(mid_here, "tp", axis=1, tiled=True)
+    chunks = []
+    for _ in range(lax.axis_size("tp")):
+        chunks.append(mid_here)
+    mid_full = jnp.concatenate(lax.all_to_all(jnp.stack(chunks), "tp", 0, 0), axis=1)
     joined = jnp.concatenate([mid_full, full_embeds], axis=1)
     attn_in = rms_rows(joined, attn_gain).astype(jnp.bfloat16)
     low_sum = accumulate_rows(attn_in, lax.all_gather(adapter_down, "tp", axis=0, tiled=True))

time: 788 us -> 719 us (0.912)
  waiting for transfers between devices: 566 us -> 516 us
  local copies, waits for them, and re-layouts: 41 us -> 21 us
    all_gather x1 -> x0, waiting for transfers between devices: 60 us -> none  [on_device(): mid_full = lax.all_gather(mid_here, 'tp', axis=1, tiled=True)]
    mul x31, local copies, waits for them, and re-layouts: 21.3 us -> 0.29 us  [combine_states(): later[0][:, None, None] * earlier[1] + later[1]]
where the time goes in v1:
time: 719 us; the launch traced here: 717 us
  waiting for transfers between devices  516 us (72%)
  blocking collectives  62.9 us (9%)
  other arithmetic  49.1 us (7%)
  matrix products  28.3 us (4%)
  starting transfers between devices  21.8 us (3%)
  local copies, waits for them, and re-layouts  21 us (3%)
  between operations  17.8 us (2%)
    reduce_scatter x1, waiting for transfers between devices, on_device(): lax.psum_scatter(mix_terms, 'tp', scatter_dimension=1, tiled=True)  88.4 us
    all_gather x1, waiting for transfers between devices, on_device(): lax.all_gather(adapter_down, 'tp', axis=0, tiled=True)  87.6 us
    reduce_scatter x1, waiting for transfers between devices, on_device(): lax.psum_scatter(attn_terms.astype(jnp.bfloat16), 'tp', scatter_dimension...  81.5 us
    ppermute x9, waiting for transfers between devices, from_behind(): return lax.ppermute(block, axis, route)  70.4 us
    all_gather x1, waiting for transfers between devices, on_device(): lax.all_gather(w_bc, 'tp', axis=0, tiled=True)  58.4 us
    all_gather x1, waiting for transfers between devices, on_device(): lax.all_gather(hidden_in, 'tp', axis=1, tiled=True)  56.6 us
    all_gather x1, waiting for transfers between devices, on_device(): lax.all_gather(embeds, 'tp', axis=1, tiled=True)  45.2 us
    all_gather x1, blocking collectives, carried_in_2(): pieces = jax.tree.map(lambda part: lax.all_gather(part, axis), value)  32.8 us
  transfers between devices with their start and end apart: 17, of which 17 were waited for; matrix products, arithmetic and copies ran while one was open for 5% of the time, Pallas kernels for 0%

profile of v1, /device:TPU:8, one launch (start us, length us, event | category | flops | bytes accessed | tf_op | source)
XLA Modules:
  0.0 717.5 jit_solution(101189813368376278)
XLA Ops:
  8.7 1.3 dynamic_slice.74
  16.8 1.4 broadcast_compare_fusion.9
  18.2 56.6 %all-gather.8.cloned.1.call-done = bf16[256,2048]{1,0:T(8,128)(2,1)} async-done(((bf16[256,256]{1,0:T(8,128)(2,1)}), bf16[256,2048]{1,0:T(8,128)(2,1)}) %all-gather.8.cloned.1.call-update) | async-done | bytes 1048592 | tf_op jit(solution)/shard_map/all_gather | solution.py:132
  74.9 1.6 fusion.6
  76.5 58.4 %all-gather.10.cloned.1.call-done = bf16[2048,256]{1,0:T(8,128)(2,1)} async-done(((bf16[256,256]{1,0:T(8,128)(2,1)}), bf16[2048,256]{1,0:T(8,128)(2,1)}) %all-gather.10.cloned.1.call-update) | async-done | bytes 1048592 | tf_op jit(solution)/shard_map/all_gather | solution.py:139
  134.8 2.2 fusion.161
  137.1 1.9 fusion.163
  139.1 1.9 collective-permute-start
  141.6 1.2 reduce-window.19
  143.5 6.0 collective-permute-done
  150.5 1.0 convolution_add_fusion
  152.0 2.0 and_and_fusion.6
  154.1 32.8 %all-gather.1 = f32[32,1,4]{2,1,0:T(1,128)S(1)} all-gather(f32[1,1,4]{2,1,0:T(1,128)S(1)} %bitcast.394), channel_id=1, replica_groups=mesh['req'=32,'tp'=8] {'req'}, dimensions={0}, use_global_device_ids=true | all-gather | bytes 528 | tf_op jit(solution)/shard_map/all_gather | solution.py:20
  187.4 1.4 convolution_bitcast_fusion.10
  189.1 20.2 %all-gather.16.cloned.1.call-done = f32[128,64,128]{2,1,0:T(8,128)} async-done(((f32[4,64,128]{2,1,0:T(8,128)}), f32[128,64,128]{2,1,0:T(8,128)}) %all-gather.16.cloned.1.call-update) | async-done | bytes 4194320 | tf_op jit(solution)/shard_map/all_gather | solution.py:20
  209.4 32.0 %while.9 = (s32[]{:T(128)}, f32[4,64,128]{2,1,0:T(8,128)S(1)}, s32[]{:T(128)}, f32[32,4]{1,0:T(8,128)S(1)}, f32[32,4,64,128]{3,2,1,0:T(8,128)}, /*index=5*/s32[]{:T(128)}, s32[]{:T(128)}) while((s32[]{:T(128)}, f32[4,64,128]{2,1,0:T(8,128)S(1)}, s32[]{:T(128)}, f32[32,4]{1,0:T(8,128)S(1)}, f32[32,4,64,128]{3,2,1,0:T(8,128)}, ...), condition=%wide.region_4.5_spmd.clone, body=%wide.region_3.4_spmd.clone.sunk | while | flops 131076 | bytes 393369 | solution.py:29
  210.4 1.0 fusion.223
  211.4 1.0 fusion.223
  214.5 1.0 fusion.223
  215.6 1.0 fusion.223
  218.7 1.0 fusion.223
  219.7 1.0 fusion.223
  220.7 1.0 fusion.223
  223.8 1.0 fusion.223
  224.9 1.0 fusion.223
  225.9 1.0 fusion.223
  229.0 1.0 fusion.223
  230.0 1.0 fusion.223
  231.1 1.0 fusion.223
  241.8 1.9 multiply_reduce_fusion
  243.7 30.1 %psum.7 = f32[256]{0:T(256)S(1)} all-reduce(f32[256]{0:T(256)S(1)} %get-tuple-element.287), channel_id=1, replica_groups=mesh['req'=32,'tp'=8] {'tp'}, use_global_device_ids=true, to_apply=%region_6.7 | all-reduce | flops 256 | bytes 2048 | tf_op jit(solution)/shard_map/psum | solution.py:211
  273.8 1.9 fusion.110
  277.2 88.4 %reduce-scatter.3.cloned.1.call-done = f32[256,256]{1,0:T(8,128)} async-done(((f32[256,2048]{1,0:T(8,128)}), f32[256,256]{1,0:T(8,128)}) %reduce-scatter.3.cloned.1.call-update) | async-done | bytes 262160 | tf_op jit(solution)/shard_map/reduce_scatter | solution.py:215
  366.5 1.1 stack.4
  367.6 3.7 all-to-all-start
  371.5 8.8 %copy.136 = bf16[4096,3,256]{0,2,1:T(8,128)(2,1)} copy(bf16[4096,3,256]{2,0,1:T(8,128)(2,1)} %param.38) | data formatting | bytes 12582912 | tf_op args[16]
  381.2 1.1 and_and_fusion.1
  382.4 1.2 multiply_cosine_fusion
  383.5 5.2 all-to-all-done
  389.3 45.2 %all-gather.12.cloned.1.call-done = bf16[256,2048]{0,1:T(8,128)(2,1)} async-done(((bf16[256,256]{0,1:T(8,128)(2,1)}), bf16[256,2048]{0,1:T(8,128)(2,1)}) %all-gather.12.cloned.1.call-update) | async-done | bytes 1048592 | tf_op jit(solution)/shard_map/all_gather | solution.py:133
  434.5 1.9 fusion.3
  436.4 87.6 %all-gather.14.cloned.1.call-done = bf16[4096,384]{1,0:T(8,128)(2,1)} async-done(((bf16[512,384]{1,0:T(8,128)(2,1)}), bf16[4096,384]{1,0:T(8,128)(2,1)}) %all-gather.14.cloned.1.call-update) | async-done | bytes 3145744 | tf_op jit(solution)/shard_map/all_gather | solution.py:223
  524.0 5.1 convolution_convert_fusion.1
  529.2 1.7 copy.138
  530.9 4.8 fusion.1
  537.0 2.1 collective-permute-start.1
  539.8 7.7 %collective-permute-done.1 = bf16[256,2,256]{0,2,1:T(8,128)(2,1)S(1)} collective-permute-done((bf16[256,2,256]{0,2,1:T(8,128)(2,1)S(1)}, bf16[256,2,256]{0,2,1:T(8,128)(2,1)S(1)}, u32[]{:S(2)}, u32[]{:S(2)}) %collective-permute-start.1) | collective-permute-done | bytes 262176 | tf_op jit(solution)/shard_map/ppermute | solution.py:15
  547.5 1.9 collective-permute-start.2
  549.7 8.1 %collective-permute-done.2 = bf16[256,2,256]{0,2,1:T(8,128)(2,1)S(1)} collective-permute-done((bf16[256,2,256]{0,2,1:T(8,128)(2,1)S(1)}, bf16[256,2,256]{0,2,1:T(8,128)(2,1)S(1)}, u32[]{:S(2)}, u32[]{:S(2)}) %collective-permute-start.2) | collective-permute-done | bytes 262176 | tf_op jit(solution)/shard_map/ppermute | solution.py:15
  557.9 1.9 collective-permute-start.3
  560.1 8.1 %collective-permute-done.3 = bf16[256,2,256]{0,2,1:T(8,128)(2,1)S(1)} collective-permute-done((bf16[256,2,256]{0,2,1:T(8,128)(2,1)S(1)}, bf16[256,2,256]{0,2,1:T(8,128)(2,1)S(1)}, u32[]{:S(2)}, u32[]{:S(2)}) %collective-permute-start.3) | collective-permute-done | bytes 262176 | tf_op jit(solution)/shard_map/ppermute | solution.py:15
  568.2 1.9 collective-permute-start.4
  570.5 8.1 %collective-permute-done.4 = bf16[256,2,256]{0,2,1:T(8,128)(2,1)S(1)} collective-permute-done((bf16[256,2,256]{0,2,1:T(8,128)(2,1)S(1)}, bf16[256,2,256]{0,2,1:T(8,128)(2,1)S(1)}, u32[]{:S(2)}, u32[]{:S(2)}) %collective-permute-start.4) | collective-permute-done | bytes 262176 | tf_op jit(solution)/shard_map/ppermute | solution.py:15
  578.6 2.1 collective-permute-start.5
  581.0 8.1 %collective-permute-done.5 = bf16[256,2,256]{0,2,1:T(8,128)(2,1)S(1)} collective-permute-done((bf16[256,2,256]{0,2,1:T(8,128)(2,1)S(1)}, bf16[256,2,256]{0,2,1:T(8,128)(2,1)S(1)}, u32[]{:S(2)}, u32[]{:S(2)}) %collective-permute-start.5) | collective-permute-done | bytes 262176 | tf_op jit(solution)/shard_map/ppermute | solution.py:15
  589.2 1.9 collective-permute-start.6
  591.4 8.1 %collective-permute-done.6 = bf16[256,2,256]{0,2,1:T(8,128)(2,1)S(1)} collective-permute-done((bf16[256,2,256]{0,2,1:T(8,128)(2,1)S(1)}, bf16[256,2,256]{0,2,1:T(8,128)(2,1)S(1)}, u32[]{:S(2)}, u32[]{:S(2)}) %collective-permute-start.6) | collective-permute-done | bytes 262176 | tf_op jit(solution)/shard_map/ppermute | solution.py:15
  599.5 1.9 collective-permute-start.7
  601.8 8.1 %collective-permute-done.7 = bf16[256,2,256]{0,2,1:T(8,128)(2,1)S(1)} collective-permute-done((bf16[256,2,256]{0,2,1:T(8,128)(2,1)S(1)}, bf16[256,2,256]{0,2,1:T(8,128)(2,1)S(1)}, u32[]{:S(2)}, u32[]{:S(2)}) %collective-permute-start.7) | collective-permute-done | bytes 262176 | tf_op jit(solution)/shard_map/ppermute | solution.py:15
  609.9 2.1 collective-permute-start.8
  612.4 7.9 %collective-permute-done.8 = bf16[256,2,256]{0,2,1:T(8,128)(2,1)S(1)} collective-permute-done((bf16[256,2,256]{0,2,1:T(8,128)(2,1)S(1)}, bf16[256,2,256]{0,2,1:T(8,128)(2,1)S(1)}, u32[]{:S(2)}, u32[]{:S(2)}) %collective-permute-start.8) | collective-permute-done | bytes 262176 | tf_op jit(solution)/shard_map/ppermute | solution.py:15
  624.5 1.4 convolution_convert_fusion
  627.5 81.5 %reduce-scatter.5.cloned.1.call-done = bf16[256,256]{1,0:T(8,128)(2,1)} async-done(((bf16[256,2048]{1,0:T(8,128)(2,1)}), bf16[256,256]{1,0:T(8,128)(2,1)}) %reduce-scatter.5.cloned.1.call-update) | async-done | bytes 131088 | tf_op jit(solution)/shard_map/reduce_scatter | solution.py:293
  709.1 1.6 add_convert_fusion
  (229 shorter events, 41.5 us)
Async XLA Ops:
  7.2 266.6 %copy-start = (bf16[256,2048]{1,0:T(8,128)(2,1)S(1)}, bf16[256,2048]{1,0:T(8,128)(2,1)}, u32[]{:S(2)}) copy-start(bf16[256,2048]{1,0:T(8,128)(2,1)} %param.36) | copy-start | bytes 3145732
  7.2 67.7 %all-gather.8.cloned.1.call-start = ((), (), s32[]{:S(2)}) async-start(), calls=%async_computation.3 | async-start | bytes 1179648 | tf_op jit(solution)/shard_map/all_gather | solution.py:132
  7.9 129.1 %copy-start.23 = (f32[2048]{0:T(1024)S(1)}, f32[2048]{0:T(1024)}, u32[]{:S(2)}) copy-start(f32[2048]{0:T(1024)} %param.25) | copy-start | bytes 24580
  7.9 126.9 %all-gather.10.cloned.1.call-start = ((), (), s32[]{:S(2)}) async-start(), calls=%async_computation.4 | async-start | bytes 1179648 | tf_op jit(solution)/shard_map/all_gather | solution.py:139
  8.7 200.7 %all-gather.16.cloned.1.call-start = ((), (), s32[]{:S(2)}) async-start(), calls=%async_computation.9 | async-start | bytes 4325376 | tf_op jit(solution)/shard_map/all_gather | solution.py:20
  74.9 62.2 %copy-start.3 = (bf16[256,2048]{1,0:T(8,128)(2,1)S(1)}, bf16[256,2048]{1,0:T(8,128)(2,1)}, u32[]{:S(2)}) copy-start(bf16[256,2048]{1,0:T(8,128)(2,1)} %all-gather.8.cloned.1.call-done) | copy-start | bytes 3145732
  137.1 4.0 copy-start.22
  137.1 4.0 copy-start.24
  137.1 4.0 copy-start.25
  139.1 10.4 %collective-permute-start = (f32[3,512]{0,1:T(8,128)S(1)}, f32[3,512]{0,1:T(8,128)S(1)}, u32[]{:S(2)}, u32[]{:S(2)}) collective-permute-start(f32[3,512]{0,1:T(8,128)S(1)} %fusion.80), channel_id=1, source_target_pairs={{0,8},{8,16},{16,24},{24,32},{32,40},{40,48},{48,56},{56,64},{64,7... | collective-permute-start | bytes 18440 | tf_op jit(solution)/shard_map/ppermute | solution.py:15
  149.8 2.0 copy-start.17
  150.4 38.3 %copy-start.21 = (f32[4]{0:T(128)S(1)}, f32[4]{0:T(128)}, u32[]{:S(2)}) copy-start(f32[4]{0:T(128)} %param.34) | copy-start | bytes 52
  151.6 214.0 %reduce-scatter.3.cloned.1.call-start = ((), (), s32[]{:S(2)}) async-start(), calls=%async_computation.5 | async-start | bytes 2359296 | tf_op jit(solution)/shard_map/reduce_scatter | solution.py:215
  241.8 32.0 %copy-start.20 = (f32[256]{0:T(256)S(1)}, f32[256]{0:T(256)}, u32[]{:S(2)}) copy-start(f32[256]{0:T(256)} %param.35) | copy-start | bytes 3076
  273.8 2.0 copy-start.19
  275.7 89.8 %copy-start.16 = (bf16[256,256]{1,0:T(8,128)(2,1)S(1)}, bf16[256,256]{1,0:T(8,128)(2,1)}, u32[]{:S(2)}) copy-start(bf16[256,256]{1,0:T(8,128)(2,1)} %param.22) | copy-start | bytes 393220
  275.7 158.8 %all-gather.12.cloned.1.call-start = ((), (), s32[]{:S(2)}) async-start(), calls=%async_computation.6 | async-start | bytes 1179648 | tf_op jit(solution)/shard_map/all_gather | solution.py:133
  276.6 247.5 %all-gather.14.cloned.1.call-start = ((), (), s32[]{:S(2)}) async-start(), calls=%async_computation.7 | async-start | bytes 3538944 | tf_op jit(solution)/shard_map/all_gather | solution.py:223
  367.6 21.2 %all-to-all-start = ((bf16[8,256,256]{2,1,0:T(8,128)(2,1)}), bf16[8,256,256]{2,1,0:T(8,128)(2,1)S(1)}, u32[]{:S(2)}, u32[]{:S(2)}) async-start(bf16[8,256,256]{2,1,0:T(8,128)(2,1)} %stack.4), calls=%async_computation.1 | async-start | bytes 2097152 | tf_op jit(solution)/shard_map/all_to_all | solution.py:220
  371.2 337.8 %reduce-scatter.5.cloned.1.call-start = ((), (), s32[]{:S(2)}) async-start(), calls=%async_computation.8 | async-start | bytes 1179648 | tf_op jit(solution)/shard_map/reduce_scatter | solution.py:293
  434.5 89.5 %copy-start.7 = (bf16[256,2048]{0,1:T(8,128)(2,1)S(1)}, bf16[256,2048]{0,1:T(8,128)(2,1)}, u32[]{:S(2)}) copy-start(bf16[256,2048]{0,1:T(8,128)(2,1)} %all-gather.12.cloned.1.call-done) | copy-start | bytes 3145732
  530.9 4.8 copy-start.14
  530.9 4.8 copy-start.18
  535.7 0.9 copy-start.2
  536.7 2.9 copy-start.13
  537.0 12.5 %copy-start.6 = (pred[256,256]{0,1:T(8,128)(4,1)S(1)}, pred[256,256]{0,1:T(8,128)(4,1)}, u32[]{:S(2)}) copy-start(pred[256,256]{0,1:T(8,128)(4,1)} %get-tuple-element.274) | copy-start | bytes 196612
  537.0 10.5 %collective-permute-start.1 = (bf16[256,2,256]{0,2,1:T(8,128)(2,1)S(1)}, bf16[256,2,256]{0,2,1:T(8,128)(2,1)S(1)}, u32[]{:S(2)}, u32[]{:S(2)}) collective-permute-start(bf16[256,2,256]{0,2,1:T(8,128)(2,1)S(1)} %pad_maximum_fusion.2), channel_id=1, source_target_pairs={{0,8},{8,16},{16,24},{24,32},{32,40},{40,48},{48,56},{56,64},{64,7... | collective-permute-start | bytes 786440 | tf_op jit(solution)/shard_map/ppermute | solution.py:15
  539.3 20.5 %copy-start.12 = (pred[256,256]{0,1:T(8,128)(4,1)S(1)}, pred[256,256]{0,1:T(8,128)(4,1)}, u32[]{:S(2)}) copy-start(pred[256,256]{0,1:T(8,128)(4,1)} %get-tuple-element.266) | copy-start | bytes 196612
  539.5 30.7 %copy-start.11 = (pred[256,256]{0,1:T(8,128)(4,1)S(1)}, pred[256,256]{0,1:T(8,128)(4,1)}, u32[]{:S(2)}) copy-start(pred[256,256]{0,1:T(8,128)(4,1)} %get-tuple-element.267) | copy-start | bytes 196612
  547.5 10.4 %collective-permute-start.2 = (bf16[256,2,256]{0,2,1:T(8,128)(2,1)S(1)}, bf16[256,2,256]{0,2,1:T(8,128)(2,1)S(1)}, u32[]{:S(2)}, u32[]{:S(2)}) collective-permute-start(bf16[256,2,256]{0,2,1:T(8,128)(2,1)S(1)} %collective-permute-done.1), channel_id=1, source_target_pairs={{0,8},{8,16},{16,24},{24,32},{32,40},{40,48},{48,56},{56,64},{64,7... | collective-permute-start | bytes 786440 | tf_op jit(solution)/shard_map/ppermute | solution.py:15
  549.4 31.3 %copy-start.10 = (pred[256,256]{0,1:T(8,128)(4,1)S(1)}, pred[256,256]{0,1:T(8,128)(4,1)}, u32[]{:S(2)}) copy-start(pred[256,256]{0,1:T(8,128)(4,1)} %get-tuple-element.268) | copy-start | bytes 196612
  557.9 10.4 %collective-permute-start.3 = (bf16[256,2,256]{0,2,1:T(8,128)(2,1)S(1)}, bf16[256,2,256]{0,2,1:T(8,128)(2,1)S(1)}, u32[]{:S(2)}, u32[]{:S(2)}) collective-permute-start(bf16[256,2,256]{0,2,1:T(8,128)(2,1)S(1)} %collective-permute-done.2), channel_id=1, source_target_pairs={{0,8},{8,16},{16,24},{24,32},{32,40},{40,48},{48,56},{56,64},{64,7... | collective-permute-start | bytes 786440 | tf_op jit(solution)/shard_map/ppermute | solution.py:15
  559.8 31.3 %copy-start.9 = (pred[256,256]{0,1:T(8,128)(4,1)S(1)}, pred[256,256]{0,1:T(8,128)(4,1)}, u32[]{:S(2)}) copy-start(pred[256,256]{0,1:T(8,128)(4,1)} %get-tuple-element.269) | copy-start | bytes 196612
  568.2 10.4 %collective-permute-start.4 = (bf16[256,2,256]{0,2,1:T(8,128)(2,1)S(1)}, bf16[256,2,256]{0,2,1:T(8,128)(2,1)S(1)}, u32[]{:S(2)}, u32[]{:S(2)}) collective-permute-start(bf16[256,2,256]{0,2,1:T(8,128)(2,1)S(1)} %collective-permute-done.3), channel_id=1, source_target_pairs={{0,8},{8,16},{16,24},{24,32},{32,40},{40,48},{48,56},{56,64},{64,7... | collective-permute-start | bytes 786440 | tf_op jit(solution)/shard_map/ppermute | solution.py:15
  570.2 31.3 %copy-start.8 = (pred[256,256]{0,1:T(8,128)(4,1)S(1)}, pred[256,256]{0,1:T(8,128)(4,1)}, u32[]{:S(2)}) copy-start(pred[256,256]{0,1:T(8,128)(4,1)} %get-tuple-element.270) | copy-start | bytes 196612
  578.6 33.5 %copy-start.5 = (pred[256,256]{0,1:T(8,128)(4,1)S(1)}, pred[256,256]{0,1:T(8,128)(4,1)}, u32[]{:S(2)}) copy-start(pred[256,256]{0,1:T(8,128)(4,1)} %get-tuple-element.272) | copy-start | bytes 196612
  578.6 10.5 %collective-permute-start.5 = (bf16[256,2,256]{0,2,1:T(8,128)(2,1)S(1)}, bf16[256,2,256]{0,2,1:T(8,128)(2,1)S(1)}, u32[]{:S(2)}, u32[]{:S(2)}) collective-permute-start(bf16[256,2,256]{0,2,1:T(8,128)(2,1)S(1)} %collective-permute-done.4), channel_id=1, source_target_pairs={{0,8},{8,16},{16,24},{24,32},{32,40},{40,48},{48,56},{56,64},{64,7... | collective-permute-start | bytes 786440 | tf_op jit(solution)/shard_map/ppermute | solution.py:15
  589.2 10.4 %collective-permute-start.6 = (bf16[256,2,256]{0,2,1:T(8,128)(2,1)S(1)}, bf16[256,2,256]{0,2,1:T(8,128)(2,1)S(1)}, u32[]{:S(2)}, u32[]{:S(2)}) collective-permute-start(bf16[256,2,256]{0,2,1:T(8,128)(2,1)S(1)} %collective-permute-done.5), channel_id=1, source_target_pairs={{0,8},{8,16},{16,24},{24,32},{32,40},{40,48},{48,56},{56,64},{64,7... | collective-permute-start | bytes 786440 | tf_op jit(solution)/shard_map/ppermute | solution.py:15
  591.1 29.2 %copy-start.15 = (pred[256,256]{0,1:T(8,128)(4,1)S(1)}, pred[256,256]{0,1:T(8,128)(4,1)}, u32[]{:S(2)}) copy-start(pred[256,256]{0,1:T(8,128)(4,1)} %get-tuple-element.273) | copy-start | bytes 196612
  599.5 10.4 %collective-permute-start.7 = (bf16[256,2,256]{0,2,1:T(8,128)(2,1)S(1)}, bf16[256,2,256]{0,2,1:T(8,128)(2,1)S(1)}, u32[]{:S(2)}, u32[]{:S(2)}) collective-permute-start(bf16[256,2,256]{0,2,1:T(8,128)(2,1)S(1)} %collective-permute-done.6), channel_id=1, source_target_pairs={{0,8},{8,16},{16,24},{24,32},{32,40},{40,48},{48,56},{56,64},{64,7... | collective-permute-start | bytes 786440 | tf_op jit(solution)/shard_map/ppermute | solution.py:15
  609.9 10.4 %collective-permute-start.8 = (bf16[256,2,256]{0,2,1:T(8,128)(2,1)S(1)}, bf16[256,2,256]{0,2,1:T(8,128)(2,1)S(1)}, u32[]{:S(2)}, u32[]{:S(2)}) collective-permute-start(bf16[256,2,256]{0,2,1:T(8,128)(2,1)S(1)} %collective-permute-done.7), channel_id=1, source_target_pairs={{0,8},{8,16},{16,24},{24,32},{32,40},{40,48},{48,56},{56,64},{64,7... | collective-permute-start | bytes 786440 | tf_op jit(solution)/shard_map/ppermute | solution.py:15
  623.2 1.2 copy-start.4
  623.7 2.2 copy-start.1
Sparse Core Ops, SparseCore 0:
  10.5 64.3 all-gather.7
  77.5 57.2 all-gather.9
  151.7 57.6 all-gather.15
  275.9 89.6 reduce-scatter.2
  368.6 65.8 all-gather.11
  437.0 87.0 all-gather.13
  626.0 82.9 reduce-scatter.4
